TPU v7x, 512 devices: a whole 4x8x8 slice. The times are simulated.
512 devices in a mesh: section: 8 (over x, z_lo), dp: 64 (over y, z_hi, core).
Axes of the slice: x: 4, y: 8, z: 8 (z_hi: 4, z_lo: 2; z = z_hi * 2 + z_lo), core: 2. Of those that a mesh axis runs over, the one named last changes fastest.
Arguments:
- saved_input: bfloat16 [8, 256, 4096], P('section', 'dp'), may hold values from -6 to 6
- grad_sent: bfloat16 [8, 256, 4096], P('section', 'dp'), may hold values from -6 to 6
- kept_blocks: int32 [8, 1664], P('section', 'dp'), may hold values from 0 to 63, as said below
- gate_blocks: bfloat16 [8, 1664, 128, 128], P('section', 'dp'), may hold values from -0.15625 to 0.15625
- up_blocks: bfloat16 [8, 1664, 128, 128], P('section', 'dp'), may hold values from -0.15625 to 0.15625
- down_blocks: bfloat16 [8, 1664, 128, 128], P('section', 'dp'), may hold values from -0.078125 to 0.078125
Outputs:
- grad_input: bfloat16 [8, 256, 4096], P('section', 'dp')
- grad_gate: bfloat16 [8, 1664, 128, 128], P('section', 'dp')
- grad_up: bfloat16 [8, 1664, 128, 128], P('section', 'dp')
- grad_down: bfloat16 [8, 1664, 128, 128], P('section', 'dp')
Inputs may be any that keep to these rules, and one draw needn't show every extreme that they name: `kept_blocks`: each device's 26 ids are different and increasing; an id is the band along the model width times 2 plus the block among that device's hidden units; bands keep unequal shares of their blocks.
All inputs are finite; a program needn't handle non-finite values.
Results may differ from a plain program's by a relative error of at most 0.019.
Values may be sent and summed in bfloat16 or wider, within the bound.
No kernel may reach another device: no remote copies, remote signals or barrier semaphores. Data moves between devices by JAX's collectives and lax.ppermute only.
A program may use at most 64 MiB of HBM per device.

v0:
```python
import jax
import jax.numpy as jnp
from jax import lax
from jax.sharding import Mesh, PartitionSpec as P

FF = 16384
ROW_AXES = ("y", "zh", "core")


def passed_along(block, axis, distance):
    devices = range(lax.axis_size(axis))
    route = [((i - distance) % len(devices), i) for i in devices]
    return lax.ppermute(block, axis, route)


def shifted(block, axis, shift):
    n = lax.axis_size(axis)
    return lax.ppermute(block, axis, [(i, (i + shift) % n) for i in range(n)])


def shifted(block, axis, shift):
    n = lax.axis_size(axis)
    return lax.ppermute(block, axis, [(i, (i + shift) % n) for i in range(n)])


def gather_rows(block):
    for axis in (("y", "zh"), "core"):
        block = lax.all_gather(block, axis, axis=1, tiled=True)
    return block


def scatter_rows(block):
    for axis in ("core", "y"):
        block = lax.psum_scatter(block, axis, scatter_dimension=0, tiled=True)
    n = lax.axis_size("zh")
    idx = lax.axis_index("zh")
    chunks = jnp.split(block, n, axis=0)
    total = None
    for k in range(1, n):
        sent = jnp.stack(chunks)[(idx - k) % n]
        got = shifted(sent, "zh", -k)
        total = got if total is None else total + got
    return total + jnp.stack(chunks)[idx]


def per_device(saved_input, grad_sent, kept_blocks, gate_blocks, up_blocks, down_blocks):
    width = saved_input.shape[2]
    block = gate_blocks.shape[2]
    bands = width // block
    n_dp = 1
    for axis in ROW_AXES:
        n_dp *= lax.axis_size(axis)
    columns = FF // n_dp // block
    ids = kept_blocks[0]
    band_ids = ids // columns
    col_ids = ids % columns
    w_gate = gate_blocks[0]
    w_up = up_blocks[0]
    w_down = down_blocks[0]
    col_onehot = (col_ids[:, None] == jnp.arange(columns, dtype=jnp.int32)[None, :]).astype(
        jnp.float32
    )
    band_onehot = (band_ids[:, None] == jnp.arange(bands, dtype=jnp.int32)[None, :]).astype(
        jnp.float32
    )

    def to_columns(partial_value):
        spread = jnp.einsum("tkc,kn->tnc", partial_value, col_onehot)
        return spread.reshape(partial_value.shape[0], columns * block)

    def pick_cols(values):
        return jnp.take(values.reshape(values.shape[0], columns, block), col_ids, axis=1)

    def pick_bands(values):
        return jnp.take(values.reshape(values.shape[0], bands, block), band_ids, axis=1)

    incoming = passed_along(grad_sent, "section", -1)
    both = gather_rows(jnp.concatenate([saved_input, incoming], axis=0))
    inputs = both[0]
    upstream = both[1]
    chosen = pick_bands(inputs)
    gate = to_columns(
        jnp.einsum("tkb,kbc->tkc", chosen, w_gate, preferred_element_type=jnp.float32)
    )
    up = to_columns(jnp.einsum("tkb,kbc->tkc", chosen, w_up, preferred_element_type=jnp.float32))
    sig = jax.nn.sigmoid(gate)
    act = gate * sig
    hidden = (act * up).astype(jnp.bfloat16)
    grad_sel = pick_bands(upstream)
    dhid = to_columns(
        jnp.einsum("tkb,kcb->tkc", grad_sel, w_down, preferred_element_type=jnp.float32)
    )
    grad_up_act = (dhid * act).astype(jnp.bfloat16)
    grad_gate_act = (dhid * up * sig * (1.0 + gate * (1.0 - sig))).astype(jnp.bfloat16)
    input_sel = chosen
    tiles_down = jnp.einsum(
        "tkc,tkb->kcb", pick_cols(hidden), grad_sel, preferred_element_type=jnp.float32
    )
    tiles_gate = jnp.einsum(
        "tkb,tkc->kbc", input_sel, pick_cols(grad_gate_act), preferred_element_type=jnp.float32
    )
    tiles_up = jnp.einsum(
        "tkb,tkc->kbc", input_sel, pick_cols(grad_up_act), preferred_element_type=jnp.float32
    )
    slots = jnp.einsum(
        "tkc,kbc->tkb", pick_cols(grad_gate_act), w_gate, preferred_element_type=jnp.float32
    )
    slots = slots + jnp.einsum(
        "tkc,kbc->tkb", pick_cols(grad_up_act), w_up, preferred_element_type=jnp.float32
    )
    spread = jnp.einsum("tkb,kr->trb", slots, band_onehot)
    whole_term = spread.reshape(grad_gate_act.shape[0], bands * block)
    summed = scatter_rows(whole_term)
    grad_input = summed.astype(jnp.bfloat16)[None]
    return (
        grad_input,
        tiles_gate.astype(jnp.bfloat16)[None],
        tiles_up.astype(jnp.bfloat16)[None],
        tiles_down.astype(jnp.bfloat16)[None],
    )


def solution(mesh):
    n_dp = mesh.shape["dp"]
    split = Mesh(
        mesh.devices.reshape(mesh.shape["section"], n_dp // 8, 4, 2), ("section",) + ROW_AXES
    )
    rows = P("section", ROW_AXES, None)
    blocks = P("section", ROW_AXES, None, None)
    return jax.shard_map(
        per_device,
        mesh=split,
        in_specs=(rows, rows, P("section", ROW_AXES), blocks, blocks, blocks),
        out_specs=(rows, blocks, blocks, blocks),
        check_vma=False,
    )
```

profile of v0, /device:TPU:4, one launch (start us, length us, event | category | flops | bytes accessed | tf_op | source)
XLA Modules:
  0.0 264.7 jit_solution(5527434780666227582)
XLA Ops:
  7.2 0.0 all-gather.3.cloned.1.call-start
  7.2 4.4 %collective-permute-start = (bf16[1,4,4096]{2,1,0:T(4,128)(2,1)}, bf16[1,4,4096]{2,1,0:T(4,128)(2,1)S(1)}, u32[]{:S(2)}, u32[]{:S(2)}) collective-permute-start(bf16[1,4,4096]{2,1,0:T(4,128)(2,1)} %param.11), channel_id=1, source_target_pairs={{64,0},{128,64},{192,128},{256,192},{320,256},{384,320},{448,384},... | collective-permute-start | bytes 98312 | tf_op jit(solution)/shard_map/ppermute | solution.py:13
  11.6 2.1 collective-permute-done
  13.7 0.8 pad_maximum_fusion.1
  14.5 0.7 copy.47
  15.2 0.0 all-gather.3.cloned.1.call-update
  15.3 0.0 all-gather.5.cloned.1.call-start
  15.3 93.7 %all-gather.3.cloned.1.call-done = bf16[2,128,4096]{2,0,1:T(2,128)(2,1)} async-done(((bf16[2,4,4096]{2,0,1:T(2,128)(2,1)}), bf16[2,128,4096]{2,0,1:T(2,128)(2,1)}) %all-gather.3.cloned.1.call-update) | async-done | bytes 2097168 | tf_op jit(solution)/shard_map/all_gather | solution.py:28
  109.0 6.2 %copy.48 = bf16[2,128,4096]{1,2,0:T(8,128)(2,1)} copy(bf16[2,128,4096]{2,0,1:T(2,128)(2,1)} %all-gather.3.cloned.1.call-done) | data formatting | bytes 4194304 | tf_op jit(solution)/shard_map/all_gather | solution.py:28
  115.2 0.0 all-gather.5.cloned.1.call-update
  115.2 0.0 reduce-scatter.3.cloned.1.call-start
  115.3 0.6 copy-done.9
  115.9 16.1 %all-gather.5.cloned.1.call-done = bf16[2,256,4096]{1,2,0:T(8,128)(2,1)} async-done(((bf16[2,128,4096]{1,2,0:T(8,128)(2,1)}), bf16[2,256,4096]{1,2,0:T(8,128)(2,1)}) %all-gather.5.cloned.1.call-update) | async-done | bytes 4194320 | tf_op jit(solution)/shard_map/all_gather | solution.py:28
  132.0 4.5 %fusion.87 = (bf16[1,256,4096]{1,2,0:T(8,128)(2,1)}, bf16[1,256,4096]{1,2,0:T(8,128)(2,1)}) fusion(bf16[2,256,4096]{1,2,0:T(8,128)(2,1)} %all-gather.5.cloned.1.call-done), kind=kLoop, calls=%fused_computation.106 | loop fusion | bytes 8388608 | tf_op jit(solution)/shard_map/slice | solution.py:80
  136.5 3.2 %copy.49 = bf16[256,32,128]{2,0,1:T(8,128)(2,1)S(1)} copy(bf16[256,32,128]{0,2,1:T(8,128)(2,1)} %bitcast.175) | data formatting | bytes 4194304 | tf_op jit(solution)/shard_map/reshape;squeeze | solution.py:75
  139.7 4.1 %copy.52 = bf16[256,32,128]{2,0,1:T(8,128)(2,1)} copy(bf16[256,32,128]{0,2,1:T(8,128)(2,1)} %bitcast.174) | data formatting | bytes 4194304 | tf_op jit(solution)/shard_map/reshape;squeeze | solution.py:75
  143.8 2.0 gather_fusion
  145.8 2.5 gather_fusion.1
  148.2 0.7 convolution_bitcast_fusion
  148.9 1.1 fusion.2
  150.0 0.1 copy-done.7
  150.1 0.7 convolution_bitcast_fusion.1
  150.7 1.1 fusion.4
  151.8 0.5 copy-done.3
  152.3 0.7 convolution_bitcast_fusion.2
  152.9 1.1 fusion.6
  154.0 0.2 fusion.68
  154.1 0.9 gather_fusion.2
  155.0 2.0 gather_fusion.3
  157.0 0.6 fusion.15
  157.7 0.8 copy-done.1
  158.5 0.2 copy-done.8
  158.7 0.7 add_bitcast_fusion
  159.3 1.1 fusion
  160.5 5.9 %copy.84 = f32[32,8,32,128]{3,1,2,0:T(8,128)} copy(f32[32,8,32,128]{3,2,1,0:T(8,128)S(1)} %bitcast.173) | data formatting | bytes 8388608
  166.4 0.0 reduce-scatter.5.cloned.1.call-start
  166.5 21.7 %reduce-scatter.3.cloned.1.call-done = f32[128,4096]{1,0:T(8,128)} async-done(((f32[256,4096]{1,0:T(8,128)}), f32[128,4096]{1,0:T(8,128)}) %reduce-scatter.3.cloned.1.call-update) | async-done | bytes 2097168 | tf_op jit(solution)/shard_map/reduce_scatter | solution.py:34
  188.3 2.0 gather_fusion.4
  190.3 3.3 %fusion.50 = bf16[1,26,128,128]{3,2,1,0:T(8,128)(2,1)} fusion(bf16[26,256,128]{2,1,0:T(8,128)(2,1)S(1)} %gather_fusion.2, pred[26]{0:T(512)(128)(4,1)S(1)} %get-tuple-element.6, bf16[26,256,128]{2,1,0:T(8,128)(2,1)} %copy-done.5, pred[26]{0:T(512)(128)(4,1)S(1)} %get-tuple-element.22), kind=kOutput, calls=%fused_computation.44 | convolution fusion | flops 220233728 | bytes 4259892 | tf_op jit(solution)/shard_map/tkb,tkc->kbc/dot_general | solution.py:99
  193.6 1.7 fusion.45
  195.4 41.3 %reduce-scatter.5.cloned.1.call-done = f32[16,4096]{1,0:T(8,128)} async-done(((f32[128,4096]{1,0:T(8,128)}), f32[16,4096]{1,0:T(8,128)}) %reduce-scatter.5.cloned.1.call-update) | async-done | bytes 262160 | tf_op jit(solution)/shard_map/reduce_scatter | solution.py:34
  236.6 1.1 slice_bitcast_fusion.3
  237.8 0.1 pad_maximum_fusion
  237.9 8.5 %collective-permute-start.2 = (f32[4,4096]{1,0:T(4,128)S(1)}, f32[4,4096]{1,0:T(4,128)S(1)}, u32[]{:S(2)}, u32[]{:S(2)}) collective-permute-start(f32[4,4096]{1,0:T(4,128)S(1)} %get-tuple-element.15), channel_id=1, source_target_pairs={{0,4},{2,6},{4,0},{6,2},{1,5},{3,7},{5,1},{7,3},{8,12},{10,14},{12... | collective-permute-start | bytes 196616 | tf_op jit(solution)/shard_map/ppermute | solution.py:23
  246.4 2.4 collective-permute-start.3
  248.8 5.5 %collective-permute-start.1 = (f32[4,4096]{1,0:T(4,128)S(1)}, f32[4,4096]{1,0:T(4,128)S(1)}, u32[]{:S(2)}, u32[]{:S(2)}) collective-permute-start(f32[4,4096]{1,0:T(4,128)S(1)} %get-tuple-element.17), channel_id=1, source_target_pairs={{0,6},{2,0},{4,2},{6,4},{1,7},{3,1},{5,3},{7,5},{8,14},{10,8},{12,... | collective-permute-start | bytes 196616 | tf_op jit(solution)/shard_map/ppermute | solution.py:23
  254.4 3.2 %fusion.40 = bf16[1,26,128,128]{3,2,1,0:T(8,128)(2,1)} fusion(bf16[26,256,128]{2,1,0:T(8,128)(2,1)} %gather_fusion.4, pred[26]{0:T(512)(128)(4,1)S(1)} %get-tuple-element.6, bf16[26,256,128]{2,1,0:T(8,128)(2,1)S(1)} %copy-done.4, pred[26]{0:T(512)(128)(4,1)S(1)} %get-tuple-element.22), kind=kOutput, calls=%fused_computation.42 | convolution fusion | flops 220233728 | bytes 4259892 | tf_op jit(solution)/shard_map/tkc,tkb->kcb/dot_general | solution.py:96
  257.5 0.7 fusion.71
  (27 shorter events, 0.1 us)
Async XLA Ops:
  7.2 141.1 %copy-start = (bf16[1,26,128,128]{3,2,1,0:T(8,128)(2,1)S(1)}, bf16[1,26,128,128]{3,2,1,0:T(8,128)(2,1)}, u32[]{:S(2)}) copy-start(bf16[1,26,128,128]{3,2,1,0:T(8,128)(2,1)} %param.13) | copy-start | bytes 2555908
  7.2 101.9 %all-gather.3.cloned.1.call-start = ((), (), s32[]{:S(2)}) async-start(), calls=%async_computation.2 | async-start | bytes 2162688 | tf_op jit(solution)/shard_map/all_gather | solution.py:28
  7.2 6.5 %collective-permute-start = (bf16[1,4,4096]{2,1,0:T(4,128)(2,1)}, bf16[1,4,4096]{2,1,0:T(4,128)(2,1)S(1)}, u32[]{:S(2)}, u32[]{:S(2)}) collective-permute-start(bf16[1,4,4096]{2,1,0:T(4,128)(2,1)} %param.11), channel_id=1, source_target_pairs={{64,0},{128,64},{192,128},{256,192},{320,256},{384,320},{448,384},... | collective-permute-start | bytes 98312 | tf_op jit(solution)/shard_map/ppermute | solution.py:13
  15.3 116.7 %all-gather.5.cloned.1.call-start = ((), (), s32[]{:S(2)}) async-start(), calls=%async_computation.3 | async-start | bytes 6291456 | tf_op jit(solution)/shard_map/all_gather | solution.py:28
  115.2 0.7 copy-start.9
  115.2 72.9 %reduce-scatter.3.cloned.1.call-start = ((), (), s32[]{:S(2)}) async-start(), calls=%async_computation.4 | async-start | bytes 6291456 | tf_op jit(solution)/shard_map/reduce_scatter | solution.py:34
  148.2 1.7 copy-start.5
  148.9 1.2 copy-start.7
  150.1 1.7 copy-start.10
  150.7 1.5 copy-start.3
  157.0 1.5 copy-start.1
  157.0 1.7 copy-start.8
  166.4 70.2 %reduce-scatter.5.cloned.1.call-start = ((), (), s32[]{:S(2)}) async-start(), calls=%async_computation.5 | async-start | bytes 2359296 | tf_op jit(solution)/shard_map/reduce_scatter | solution.py:34
  190.3 3.3 %copy-start.2 = (bf16[26,256,128]{2,1,0:T(8,128)(2,1)S(1)}, bf16[26,256,128]{2,1,0:T(8,128)(2,1)}, u32[]{:S(2)}) copy-start(bf16[26,256,128]{2,1,0:T(8,128)(2,1)} %gather_fusion.3) | copy-start | bytes 5111812
  190.3 3.3 %copy-start.6 = (bf16[26,256,128]{2,1,0:T(8,128)(2,1)S(1)}, bf16[26,256,128]{2,1,0:T(8,128)(2,1)}, u32[]{:S(2)}) copy-start(bf16[26,256,128]{2,1,0:T(8,128)(2,1)} %copy-done.5) | copy-start | bytes 5111812
  193.6 60.7 %copy-start.4 = (bf16[26,256,128]{2,1,0:T(8,128)(2,1)S(1)}, bf16[26,256,128]{2,1,0:T(8,128)(2,1)}, u32[]{:S(2)}) copy-start(bf16[26,256,128]{2,1,0:T(8,128)(2,1)} %gather_fusion) | copy-start | bytes 5111812
  237.9 19.7 %collective-permute-start.2 = (f32[4,4096]{1,0:T(4,128)S(1)}, f32[4,4096]{1,0:T(4,128)S(1)}, u32[]{:S(2)}, u32[]{:S(2)}) collective-permute-start(f32[4,4096]{1,0:T(4,128)S(1)} %get-tuple-element.15), channel_id=1, source_target_pairs={{0,4},{2,6},{4,0},{6,2},{1,5},{3,7},{5,1},{7,3},{8,12},{10,14},{12... | collective-permute-start | bytes 196616 | tf_op jit(solution)/shard_map/ppermute | solution.py:23
  246.4 11.2 %collective-permute-start.3 = (f32[4,4096]{1,0:T(4,128)S(1)}, f32[4,4096]{1,0:T(4,128)S(1)}, u32[]{:S(2)}, u32[]{:S(2)}) collective-permute-start(f32[4,4096]{1,0:T(4,128)S(1)} %get-tuple-element.16), channel_id=1, source_target_pairs={{0,2},{2,4},{4,6},{6,0},{1,3},{3,5},{5,7},{7,1},{8,10},{10,12},{12... | collective-permute-start | bytes 196616 | tf_op jit(solution)/shard_map/ppermute | solution.py:23
  248.8 8.7 %collective-permute-start.1 = (f32[4,4096]{1,0:T(4,128)S(1)}, f32[4,4096]{1,0:T(4,128)S(1)}, u32[]{:S(2)}, u32[]{:S(2)}) collective-permute-start(f32[4,4096]{1,0:T(4,128)S(1)} %get-tuple-element.17), channel_id=1, source_target_pairs={{0,6},{2,0},{4,2},{6,4},{1,7},{3,1},{5,3},{7,5},{8,14},{10,8},{12,... | collective-permute-start | bytes 196616 | tf_op jit(solution)/shard_map/ppermute | solution.py:23
Sparse Core Ops, SparseCore 0:
  15.4 93.6 all-gather.2
  115.3 16.5 all-gather.4
  166.5 21.5 reduce-scatter.2
  191.1 45.4 reduce-scatter.4
where the time goes:
time: 265 us
  waiting for transfers between devices  175 us (66%)
  local copies, waits for them, and re-layouts  37.3 us (14%)
  starting transfers between devices  21 us (8%)
  matrix products  15.8 us (6%)
  between operations  14 us (5%)
    all_gather x2, waiting for transfers between devices, gather_rows(): block = lax.all_gather(block, axis, axis=1, tiled=True)  110 us
    reduce_scatter x2, waiting for transfers between devices, scatter_rows(): block = lax.psum_scatter(block, axis, scatter_dimension=0, tiled=True)  63 us
    ppermute x3, starting transfers between devices, shifted(): return lax.ppermute(block, axis, [(i, (i + shift) % n) for i in range(n)])  16.5 us
    unnamed x23, local copies, waits for them, and re-layouts  8.1 us
    another operation x2, local copies, waits for them, and re-layouts, pick_bands(): values.reshape(values.shape[0], bands, block)  7.28 us
    all_gather x1, local copies, waits for them, and re-layouts, gather_rows(): block = lax.all_gather(block, axis, axis=1, tiled=True)  6.16 us
  transfers between devices with their start and end apart: 8, of which 5 were waited for; matrix products, arithmetic and copies ran while one was open for 4% of the time, Pallas kernels for 0%

commit v1 on v0

--- a/solution.py
+++ b/solution.py
@@ -25,7 +25,9 @@
 
 def gather_rows(block):
     for axis in (("y", "zh"), "core"):
-        block = lax.all_gather(block, axis, axis=1, tiled=True)
+        block = jnp.concatenate(
+            lax.all_to_all(jnp.stack([block] * lax.axis_size(axis)), axis, 0, 0), axis=1
+        )
     return block
 
 

time: 265 us -> 248 us (0.936)
  the two profiles are of different devices: /device:TPU:4 before, /device:TPU:2 now
where the time goes in v1:
time: 248 us
  waiting for transfers between devices  117 us (47%)
  local copies, waits for them, and re-layouts  47.5 us (19%)
  starting transfers between devices  36.8 us (15%)
  matrix products  15.8 us (6%)
  between operations  14.4 us (6%)
  blocking collectives  8.48 us (3%)
  other arithmetic  7.45 us (3%)
    reduce_scatter x2, waiting for transfers between devices, scatter_rows(): block = lax.psum_scatter(block, axis, scatter_dimension=0, tiled=True)  62.7 us
    all_to_all x1, waiting for transfers between devices, gather_rows(): lax.all_to_all(jnp.stack([block] * lax.axis_size(axis)), axis, 0, 0)  52.5 us
    slice x1, local copies, waits for them, and re-layouts, per_device(): upstream = both[1]  21.3 us
    ppermute x3, starting transfers between devices, shifted(): return lax.ppermute(block, axis, [(i, (i + shift) % n) for i in range(n)])  16.6 us
    all_to_all x1, starting transfers between devices, gather_rows(): lax.all_to_all(jnp.stack([block] * lax.axis_size(axis)), axis, 0, 0)  15.7 us
    unnamed x27, local copies, waits for them, and re-layouts  9.29 us
    all_to_all x1, blocking collectives, gather_rows(): lax.all_to_all(jnp.stack([block] * lax.axis_size(axis)), axis, 0, 0)  8.48 us
    another operation x1, other arithmetic, gather_rows(): jnp.stack([block] * lax.axis_size(axis))  5.73 us
  transfers between devices with their start and end apart: 7, of which 4 were waited for; matrix products, arithmetic and copies ran while one was open for 4% of the time, Pallas kernels for 0%

profile of v1, /device:TPU:2, one launch (start us, length us, event | category | flops | bytes accessed | tf_op | source)
XLA Modules:
  0.0 247.8 jit_solution(10372976451052880842)
XLA Ops:
  7.2 4.4 %collective-permute-start = (bf16[1,4,4096]{2,1,0:T(4,128)(2,1)}, bf16[1,4,4096]{2,1,0:T(4,128)(2,1)S(1)}, u32[]{:S(2)}, u32[]{:S(2)}) collective-permute-start(bf16[1,4,4096]{2,1,0:T(4,128)(2,1)} %param.11), channel_id=1, source_target_pairs={{64,0},{128,64},{192,128},{256,192},{320,256},{384,320},{448,384},... | collective-permute-start | bytes 98312 | tf_op jit(solution)/shard_map/ppermute | solution.py:13
  11.6 2.1 collective-permute-done
  13.7 0.8 pad_maximum_fusion.2
  14.5 0.1 copy.33
  14.6 3.4 %stack.14 = bf16[32,2,4,4096]{3,1,2,0:T(2,128)(2,1)} broadcast(bf16[2,4,4096]{2,0,1:T(2,128)(2,1)S(1)} %copy.33), dimensions={1,2,3} | broadcast | bytes 2162688 | tf_op jit(solution)/shard_map/stack | solution.py:29
  18.0 15.7 %all-to-all-start = ((bf16[32,2,4,4096]{3,1,2,0:T(2,128)(2,1)}), bf16[32,2,4,4096]{3,1,2,0:T(2,128)(2,1)S(1)}, u32[]{:S(2)}, u32[]{:S(2)}) async-start(bf16[32,2,4,4096]{3,1,2,0:T(2,128)(2,1)} %stack.14), calls=%async_computation | async-start | bytes 4194304 | tf_op jit(solution)/shard_map/all_to_all | solution.py:29
  33.7 0.0 reduce-scatter.3.cloned.1.call-start
  33.9 52.5 %all-to-all-done = bf16[32,2,4,4096]{3,1,2,0:T(2,128)(2,1)S(1)} async-done(((bf16[32,2,4,4096]{3,1,2,0:T(2,128)(2,1)}), bf16[32,2,4,4096]{3,1,2,0:T(2,128)(2,1)S(1)}, u32[]{:S(2)}, u32[]{:S(2)}) %all-to-all-start) | async-done | bytes 2097184 | tf_op jit(solution)/shard_map/all_to_all | solution.py:29
  86.4 5.7 %pad_maximum_fusion = bf16[2,2,128,4096]{3,1,2,0:T(2,128)(2,1)} fusion(bf16[1,2,128,4096]{3,1,2,0:T(2,128)(2,1)S(1)} %bitcast.183), kind=kLoop, calls=%fused_computation.8 | loop fusion | flops 2097152 | bytes 6291456 | tf_op jit(solution)/shard_map/stack | solution.py:29
  92.1 8.5 %all_to_all.10 = bf16[2,2,128,4096]{3,1,2,0:T(2,128)(2,1)S(1)} all-to-all(bf16[2,2,128,4096]{3,1,2,0:T(2,128)(2,1)} %pad_maximum_fusion), channel_id=1, replica_groups=mesh['section'=8,'y'=8,'zh'=4,'core'=2] {'core'}, dimensions={0} | all-to-all | bytes 8388608 | tf_op jit(solution)/shard_map/all_to_all | solution.py:29
  100.6 21.3 %slice_reduce_fusion.1 = (bf16[2,128,4096]{2,1,0:T(8,128)(2,1)S(1)}, bf16[2,128,4096]{2,1,0:T(8,128)(2,1)}) fusion(bf16[2,2,128,4096]{3,0,2,1:T(2,128)(2,1)S(1)} %bitcast.180), kind=kLoop, calls=%fused_computation.7 | loop fusion | bytes 8388608 | tf_op jit(solution)/shard_map/slice | solution.py:82
  121.8 0.5 copy.49
  122.3 0.8 copy.34
  123.2 0.8 copy-done.3
  123.9 0.5 copy.50
  124.4 2.2 copy.37
  126.6 2.0 gather_fusion
  128.6 2.5 gather_fusion.1
  131.1 0.7 convolution_bitcast_fusion
  131.7 1.1 fusion.2
  132.8 0.1 copy-done.8
  132.9 0.7 convolution_bitcast_fusion.1
  133.6 1.1 fusion.4
  134.6 0.5 copy-done.4
  135.1 0.6 convolution_bitcast_fusion.2
  135.7 1.1 fusion.6
  136.8 0.2 fusion.68
  137.0 0.9 gather_fusion.2
  137.8 2.0 gather_fusion.3
  139.8 0.6 fusion.15
  140.5 0.8 copy-done.1
  141.3 0.2 copy-done.9
  141.5 0.7 add_bitcast_fusion
  142.2 1.1 fusion
  143.3 6.0 %copy.71 = f32[32,8,32,128]{3,1,2,0:T(8,128)} copy(f32[32,8,32,128]{3,2,1,0:T(8,128)S(1)} %bitcast.182) | data formatting | bytes 8388608
  149.3 0.0 reduce-scatter.5.cloned.1.call-start
  149.3 21.3 %reduce-scatter.3.cloned.1.call-done = f32[128,4096]{1,0:T(8,128)} async-done(((f32[256,4096]{1,0:T(8,128)}), f32[128,4096]{1,0:T(8,128)}) %reduce-scatter.3.cloned.1.call-update) | async-done | bytes 2097168 | tf_op jit(solution)/shard_map/reduce_scatter | solution.py:36
  170.8 2.0 gather_fusion.4
  172.8 3.3 %fusion.50 = bf16[1,26,128,128]{3,2,1,0:T(8,128)(2,1)} fusion(bf16[26,256,128]{2,1,0:T(8,128)(2,1)S(1)} %gather_fusion.2, pred[26]{0:T(512)(128)(4,1)S(1)} %get-tuple-element.8, bf16[26,256,128]{2,1,0:T(8,128)(2,1)} %copy-done.6, pred[26]{0:T(512)(128)(4,1)S(1)} %get-tuple-element.22), kind=kOutput, calls=%fused_computation.47 | convolution fusion | flops 220233728 | bytes 4259892 | tf_op jit(solution)/shard_map/tkb,tkc->kbc/dot_general | solution.py:101
  176.1 1.7 fusion.45
  177.8 41.4 %reduce-scatter.5.cloned.1.call-done = f32[16,4096]{1,0:T(8,128)} async-done(((f32[128,4096]{1,0:T(8,128)}), f32[16,4096]{1,0:T(8,128)}) %reduce-scatter.5.cloned.1.call-update) | async-done | bytes 262160 | tf_op jit(solution)/shard_map/reduce_scatter | solution.py:36
  219.2 1.1 slice_bitcast_fusion.3
  220.3 0.1 pad_maximum_fusion.1
  220.4 8.7 %collective-permute-start.2 = (f32[4,4096]{1,0:T(4,128)S(1)}, f32[4,4096]{1,0:T(4,128)S(1)}, u32[]{:S(2)}, u32[]{:S(2)}) collective-permute-start(f32[4,4096]{1,0:T(4,128)S(1)} %get-tuple-element.15), channel_id=1, source_target_pairs={{0,4},{2,6},{4,0},{6,2},{1,5},{3,7},{5,1},{7,3},{8,12},{10,14},{12... | collective-permute-start | bytes 196616 | tf_op jit(solution)/shard_map/ppermute | solution.py:23
  229.1 2.3 collective-permute-start.3
  231.4 5.7 %collective-permute-start.1 = (f32[4,4096]{1,0:T(4,128)S(1)}, f32[4,4096]{1,0:T(4,128)S(1)}, u32[]{:S(2)}, u32[]{:S(2)}) collective-permute-start(f32[4,4096]{1,0:T(4,128)S(1)} %get-tuple-element.17), channel_id=1, source_target_pairs={{0,6},{2,0},{4,2},{6,4},{1,7},{3,1},{5,3},{7,5},{8,14},{10,8},{12,... | collective-permute-start | bytes 196616 | tf_op jit(solution)/shard_map/ppermute | solution.py:23
  237.1 3.2 %fusion.40 = bf16[1,26,128,128]{3,2,1,0:T(8,128)(2,1)} fusion(bf16[26,256,128]{2,1,0:T(8,128)(2,1)} %gather_fusion.4, pred[26]{0:T(512)(128)(4,1)S(1)} %get-tuple-element.8, bf16[26,256,128]{2,1,0:T(8,128)(2,1)S(1)} %copy-done.5, pred[26]{0:T(512)(128)(4,1)S(1)} %get-tuple-element.22), kind=kOutput, calls=%fused_computation.45 | convolution fusion | flops 220233728 | bytes 4259892 | tf_op jit(solution)/shard_map/tkc,tkb->kcb/dot_general | solution.py:98
  240.3 0.7 fusion.71
  (29 shorter events, 0.1 us)
Async XLA Ops:
  7.2 123.9 %copy-start = (bf16[1,26,128,128]{3,2,1,0:T(8,128)(2,1)S(1)}, bf16[1,26,128,128]{3,2,1,0:T(8,128)(2,1)}, u32[]{:S(2)}) copy-start(bf16[1,26,128,128]{3,2,1,0:T(8,128)(2,1)} %param.13) | copy-start | bytes 2555908
  7.2 6.5 %collective-permute-start = (bf16[1,4,4096]{2,1,0:T(4,128)(2,1)}, bf16[1,4,4096]{2,1,0:T(4,128)(2,1)S(1)}, u32[]{:S(2)}, u32[]{:S(2)}) collective-permute-start(bf16[1,4,4096]{2,1,0:T(4,128)(2,1)} %param.11), channel_id=1, source_target_pairs={{64,0},{128,64},{192,128},{256,192},{320,256},{384,320},{448,384},... | collective-permute-start | bytes 98312 | tf_op jit(solution)/shard_map/ppermute | solution.py:13
  18.0 15.8 %copy-start.10 = (s32[1,26]{1,0:T(1,128)S(1)}, s32[1,26]{1,0:T(1,128)}, u32[]{:S(2)}) copy-start(s32[1,26]{1,0:T(1,128)} %param.12) | copy-start | bytes 316
  18.0 68.4 %all-to-all-start = ((bf16[32,2,4,4096]{3,1,2,0:T(2,128)(2,1)}), bf16[32,2,4,4096]{3,1,2,0:T(2,128)(2,1)S(1)}, u32[]{:S(2)}, u32[]{:S(2)}) async-start(bf16[32,2,4,4096]{3,1,2,0:T(2,128)(2,1)} %stack.14), calls=%async_computation | async-start | bytes 4194304 | tf_op jit(solution)/shard_map/all_to_all | solution.py:29
  33.7 136.9 %reduce-scatter.3.cloned.1.call-start = ((), (), s32[]{:S(2)}) async-start(), calls=%async_computation.4 | async-start | bytes 6291456 | tf_op jit(solution)/shard_map/reduce_scatter | solution.py:36
  122.3 1.6 copy-start.3
  131.0 2.5 %copy-start.6 = (bf16[26,256,128]{2,1,0:T(8,128)(2,1)}, bf16[26,256,128]{2,1,0:T(8,128)(2,1)S(1)}, u32[]{:S(2)}) copy-start(bf16[26,256,128]{2,1,0:T(8,128)(2,1)S(1)} %gather_fusion.1) | copy-start | bytes 5111812
  131.7 1.2 copy-start.8
  132.9 1.7 copy-start.11
  133.6 1.5 copy-start.4
  139.8 1.5 copy-start.1
  139.8 1.7 copy-start.9
  149.3 69.9 %reduce-scatter.5.cloned.1.call-start = ((), (), s32[]{:S(2)}) async-start(), calls=%async_computation.5 | async-start | bytes 2359296 | tf_op jit(solution)/shard_map/reduce_scatter | solution.py:36
  172.8 3.3 %copy-start.2 = (bf16[26,256,128]{2,1,0:T(8,128)(2,1)S(1)}, bf16[26,256,128]{2,1,0:T(8,128)(2,1)}, u32[]{:S(2)}) copy-start(bf16[26,256,128]{2,1,0:T(8,128)(2,1)} %gather_fusion.3) | copy-start | bytes 5111812
  172.8 3.3 %copy-start.7 = (bf16[26,256,128]{2,1,0:T(8,128)(2,1)S(1)}, bf16[26,256,128]{2,1,0:T(8,128)(2,1)}, u32[]{:S(2)}) copy-start(bf16[26,256,128]{2,1,0:T(8,128)(2,1)} %copy-done.6) | copy-start | bytes 5111812
  176.1 61.0 %copy-start.5 = (bf16[26,256,128]{2,1,0:T(8,128)(2,1)S(1)}, bf16[26,256,128]{2,1,0:T(8,128)(2,1)}, u32[]{:S(2)}) copy-start(bf16[26,256,128]{2,1,0:T(8,128)(2,1)} %gather_fusion) | copy-start | bytes 5111812
  220.4 19.8 %collective-permute-start.2 = (f32[4,4096]{1,0:T(4,128)S(1)}, f32[4,4096]{1,0:T(4,128)S(1)}, u32[]{:S(2)}, u32[]{:S(2)}) collective-permute-start(f32[4,4096]{1,0:T(4,128)S(1)} %get-tuple-element.15), channel_id=1, source_target_pairs={{0,4},{2,6},{4,0},{6,2},{1,5},{3,7},{5,1},{7,3},{8,12},{10,14},{12... | collective-permute-start | bytes 196616 | tf_op jit(solution)/shard_map/ppermute | solution.py:23
  229.1 11.2 %collective-permute-start.3 = (f32[4,4096]{1,0:T(4,128)S(1)}, f32[4,4096]{1,0:T(4,128)S(1)}, u32[]{:S(2)}, u32[]{:S(2)}) collective-permute-start(f32[4,4096]{1,0:T(4,128)S(1)} %get-tuple-element.16), channel_id=1, source_target_pairs={{0,2},{2,4},{4,6},{6,0},{1,3},{3,5},{5,7},{7,1},{8,10},{10,12},{12... | collective-permute-start | bytes 196616 | tf_op jit(solution)/shard_map/ppermute | solution.py:23
  231.4 8.8 %collective-permute-start.1 = (f32[4,4096]{1,0:T(4,128)S(1)}, f32[4,4096]{1,0:T(4,128)S(1)}, u32[]{:S(2)}, u32[]{:S(2)}) collective-permute-start(f32[4,4096]{1,0:T(4,128)S(1)} %get-tuple-element.17), channel_id=1, source_target_pairs={{0,6},{2,0},{4,2},{6,4},{1,7},{3,1},{5,3},{7,5},{8,14},{10,8},{12,... | collective-permute-start | bytes 196616 | tf_op jit(solution)/shard_map/ppermute | solution.py:23
Sparse Core Ops, SparseCore 0:
  149.4 21.2 reduce-scatter.2
  173.7 45.4 reduce-scatter.4
